TPU v7x, 256 devices: a whole 4x4x8 slice. The times are simulated.
256 devices in a mesh: grp: 4 (over x), tok: 8 (over z), mdl: 8 (over y, core).
Axes of the slice: x: 4, y: 4, z: 8, core: 2. Of those that a mesh axis runs over, the one named last changes fastest.
Arguments:
- hidden_in: bfloat16 [4, 1024, 5120], P('grp', 'tok', 'mdl'), may hold values from -8 to 8
- seg_ids: int32 [4, 1024], replicated, may hold values from 0 to 3, never falling along the last dimension, each value on 1 to 768 neighbouring positions
- request_prefix: int32 [4, 4], replicated, may hold values from 0 to 1
- page_table: int32 [32], replicated, may hold values from 0 to 31, each once
- prefix_cache: bfloat16 [32, 256, 8, 256], P(('grp', 'mdl'), None, 'tok'), may hold values from -200 to 200
- attn_gain: float32 [5120], P('mdl'), may hold values from 0.1 to 1.9
- w_query: bfloat16 [5120, 5120], P('mdl', 'tok'), may hold values from -0.078125 to 0.078125
- w_key: bfloat16 [5120, 1024], P('mdl', 'tok'), may hold values from -0.25 to 0.25
- w_value: bfloat16 [5120, 1024], P('mdl', 'tok'), may hold values from -0.078125 to 0.078125
- w_out: bfloat16 [5120, 5120], P('tok', 'mdl'), may hold values from -0.078125 to 0.078125
- ffn_gain: float32 [5120], P('mdl'), may hold values from 0.1 to 1.9
- w_gate: bfloat16 [5120, 14336], P('mdl', 'tok'), may hold values from -0.078125 to 0.078125
- w_up: bfloat16 [5120, 14336], P('mdl', 'tok'), may hold values from -0.078125 to 0.078125
- w_down: bfloat16 [14336, 5120], P('tok', 'mdl'), may hold values from -0.046875 to 0.046875
- final_gain: float32 [5120], replicated, may hold values from 0.1 to 1.9
- lm_head: bfloat16 [76800, 5120], P(('grp', 'tok', 'mdl')), may hold values from -0.25 to 0.25
Outputs:
- hidden_out: bfloat16 [4, 1024, 5120], P('grp', 'tok', 'mdl')
- new_kv: bfloat16 [4, 1024, 8, 256], P('grp', 'mdl', 'tok')
- req_norm: float32 [4, 4], P('grp')
- max_logit: float32 [4, 4], replicated
- logits: float32 [16, 76800], P(None, ('grp', 'tok', 'mdl'))
Inputs may be any that keep to these rules, and one draw needn't show every extreme that they name: `seg_ids`: requests of a group are contiguous, in order, and none is empty. `page_table`: each physical slot holds exactly one logical page.
All inputs are finite; a program needn't handle non-finite values.
Results may differ from a plain program's by a relative error of at most 0.024.
Values may be sent and summed in bfloat16 or wider, within the bound.
No kernel may reach another device: no remote copies, remote signals or barrier semaphores. Data moves between devices by JAX's collectives and lax.ppermute only.
A program may use at most 128 MiB of HBM per device.

v0:
```python
import jax
import jax.numpy as jnp
from jax import lax
from jax.sharding import PartitionSpec as P

PREFIX = 4096
PAGE = 256
EPS = 1e-06
THETA = 1000000.0
NEG = -1e30


def rotate(tensor, positions):
    half_dim = tensor.shape[-1] // 2
    frequency = THETA ** (-(jnp.arange(half_dim, dtype=jnp.float32) * 2.0 / tensor.shape[-1]))
    angles = positions.astype(jnp.float32)[:, None] * frequency[None, :]
    cosine = jnp.cos(angles)[:, None, :]
    sine_part = jnp.sin(angles)[:, None, :]
    first_part = tensor[..., :half_dim]
    second = tensor[..., half_dim:]
    return jnp.concatenate(
        [first_part * cosine - second * sine_part, second * cosine + first_part * sine_part], -1
    )


def on_device(
    hidden_in,
    seg_ids,
    request_prefix,
    page_table,
    prefix_cache,
    attn_gain,
    w_query,
    w_key,
    w_value,
    w_out,
    ffn_gain,
    w_gate,
    w_up,
    w_down,
    final_gain,
    lm_head,
):
    groups_total = seg_ids.shape[0]
    seq_len = seg_ids.shape[1]
    req_count = request_prefix.shape[1]
    tok_rows = hidden_in.shape[1]
    feat_dev = hidden_in.shape[2]
    model_width = feat_dev * lax.axis_size("mdl")
    head_dim = prefix_cache.shape[3] // 2
    kv_dev = prefix_cache.shape[2]
    heads_dev = w_query.shape[1] // head_dim
    group_size = heads_dev // kv_dev
    page_len = prefix_cache.shape[1]
    slot_total = page_table.shape[0]
    rows_mdl = seq_len // lax.axis_size("mdl")
    group_idx = lax.axis_index("grp")
    tok_idx = lax.axis_index("tok")
    mdl_idx = lax.axis_index("mdl")
    score_scale = head_dim ** (-0.5)
    tokens = hidden_in[0].astype(jnp.float32)
    squares = lax.psum(jnp.sum(tokens * tokens, -1), "mdl")
    normed = (tokens * lax.rsqrt(squares[:, None] / model_width + EPS) * attn_gain).astype(
        jnp.bfloat16
    )
    w_joined = jnp.concatenate([w_query, w_key, w_value], 1)
    partial_qkv = jnp.dot(
        lax.all_gather(normed, "tok", axis=0, tiled=True),
        w_joined,
        preferred_element_type=jnp.float32,
    )
    qkv_rows = lax.psum_scatter(partial_qkv, "mdl", scatter_dimension=0, tiled=True)
    q_cols = heads_dev * head_dim
    kv_cols = kv_dev * head_dim
    queries = qkv_rows[:, :q_cols].reshape(rows_mdl, heads_dev, head_dim)
    key_rows = qkv_rows[:, q_cols : q_cols + kv_cols].reshape(rows_mdl, kv_dev, head_dim)
    value_rows = qkv_rows[:, q_cols + kv_cols :].reshape(rows_mdl, kv_dev, head_dim)
    seg_row = lax.dynamic_index_in_dim(seg_ids, group_idx, 0, keepdims=False)
    prefix_row = lax.dynamic_index_in_dim(request_prefix, group_idx, 0, keepdims=False)
    requests = jnp.arange(req_count, dtype=jnp.int32)
    member = seg_row[:, None] == requests[None, :]
    counts = jnp.sum(member.astype(jnp.int32), 0)
    offsets = jnp.cumsum(counts) - counts
    row_start = mdl_idx * rows_mdl
    my_rows = row_start + jnp.arange(rows_mdl, dtype=jnp.int32)
    my_seg = lax.dynamic_slice_in_dim(seg_row, row_start, rows_mdl)
    my_member = my_seg[:, None] == requests[None, :]
    positions = PREFIX + my_rows - jnp.sum(jnp.where(my_member, offsets[None, :], 0), 1)
    my_prefix = jnp.sum(jnp.where(my_member, prefix_row[None, :], 0), 1)
    q_rot = (
        rotate(queries, positions)
        .astype(jnp.bfloat16)
        .reshape(rows_mdl, kv_dev, group_size, head_dim)
    )
    k_rot = rotate(key_rows, positions).astype(jnp.bfloat16)
    appended = jnp.concatenate([k_rot, value_rows.astype(jnp.bfloat16)], -1)
    suffix = lax.all_gather(appended, "mdl", axis=0, tiled=True)
    every_row = jnp.arange(seq_len, dtype=jnp.int32)
    suffix_ok = ((seg_row[None, :] == my_seg[:, None]) & (every_row[None, :] <= my_rows[:, None]))[
        :, None, None, :
    ]
    suffix_scores = (
        jnp.einsum(
            "rcgd,tcd->rcgt", q_rot, suffix[..., :head_dim], preferred_element_type=jnp.float32
        )
        * score_scale
    )
    suffix_scores = jnp.where(suffix_ok, suffix_scores, NEG)
    row_max = jnp.max(suffix_scores, -1)
    suffix_weights = jnp.where(suffix_ok, jnp.exp(suffix_scores - row_max[..., None]), 0.0)
    row_total = jnp.sum(suffix_weights, -1)
    mixed = jnp.einsum(
        "rcgt,tcd->rcgd",
        suffix_weights.astype(jnp.bfloat16),
        suffix[..., head_dim:],
        preferred_element_type=jnp.float32,
    )
    slot_ids = jnp.arange(slot_total, dtype=jnp.int32)
    pages_each = PREFIX // PAGE
    slot_prefix = jnp.sum(
        jnp.where(page_table[None, :] == slot_ids[:, None], (slot_ids // pages_each)[None, :], 0), 1
    )
    piece = lax.all_gather(prefix_cache, ("grp", "mdl"), axis=0, tiled=True)
    page_count = piece.shape[0]
    key_prefix = jnp.repeat(slot_prefix, page_len)
    allowed = (my_prefix[:, None] == key_prefix[None, :])[:, None, None, :]
    flat_pages = piece.reshape(page_count * page_len, kv_dev, 2 * head_dim)
    scores = (
        jnp.einsum(
            "rcgd,kcd->rcgk", q_rot, flat_pages[..., :head_dim], preferred_element_type=jnp.float32
        )
        * score_scale
    )
    scores = jnp.where(allowed, scores, NEG)
    new_max = jnp.maximum(row_max, jnp.max(scores, -1))
    factor = jnp.exp(row_max - new_max)
    page_weights = jnp.where(allowed, jnp.exp(scores - new_max[..., None]), 0.0)
    new_total = row_total * factor + jnp.sum(page_weights, -1)
    new_mixed = mixed * factor[..., None] + jnp.einsum(
        "rcgk,kcd->rcgd",
        page_weights.astype(jnp.bfloat16),
        flat_pages[..., head_dim:],
        preferred_element_type=jnp.float32,
    )
    attended = (
        (new_mixed / new_total[..., None])
        .astype(jnp.bfloat16)
        .reshape(rows_mdl, heads_dev * head_dim)
    )
    partial_out = jnp.dot(
        lax.all_gather(attended, "mdl", axis=0, tiled=True),
        w_out,
        preferred_element_type=jnp.float32,
    )
    residual = tokens + lax.psum_scatter(
        partial_out.astype(jnp.bfloat16), "tok", scatter_dimension=0, tiled=True
    ).astype(jnp.float32)
    squares_ffn = lax.psum(jnp.sum(residual * residual, -1), "mdl")
    ffn_input = (residual * lax.rsqrt(squares_ffn[:, None] / model_width + EPS) * ffn_gain).astype(
        jnp.bfloat16
    )
    w_pair = jnp.concatenate([w_gate, w_up], 1)
    ff_dev = w_gate.shape[1]
    partial_ffn = jnp.dot(
        lax.all_gather(ffn_input, "tok", axis=0, tiled=True),
        w_pair,
        preferred_element_type=jnp.float32,
    )
    summed = lax.psum_scatter(
        partial_ffn.astype(jnp.bfloat16), "mdl", scatter_dimension=0, tiled=True
    ).astype(jnp.float32)
    activated = (jax.nn.silu(summed[:, :ff_dev]) * summed[:, ff_dev:]).astype(jnp.bfloat16)
    partial_down = jnp.dot(
        lax.all_gather(activated, "mdl", axis=0, tiled=True),
        w_down,
        preferred_element_type=jnp.float32,
    )
    final_rows = residual + lax.psum_scatter(
        partial_down.astype(jnp.bfloat16), "tok", scatter_dimension=0, tiled=True
    ).astype(jnp.float32)
    tok_start = tok_idx * tok_rows
    my_tok_rows = tok_start + jnp.arange(tok_rows, dtype=jnp.int32)
    tok_seg = lax.dynamic_slice_in_dim(seg_row, tok_start, tok_rows)
    row_squares = jnp.sum(final_rows * final_rows, -1)
    req_squares = jnp.sum(
        jnp.where(tok_seg[:, None] == requests[None, :], row_squares[:, None], 0.0), 0
    )
    ends = offsets + counts - 1
    picked = ends[:, None] == my_tok_rows[None, :]
    last_part = jnp.sum(jnp.where(picked[:, :, None], final_rows[None, :, :], 0.0), 1)
    last_squares = jnp.sum(last_part * last_part, -1)
    packed = jnp.concatenate([last_part, req_squares[:, None], last_squares[:, None]], 1)
    packed = lax.psum(packed, "tok")
    blocks = lax.all_gather(packed, "mdl", axis=0, tiled=False)
    mdl_count = blocks.shape[0]
    last_rows = jnp.transpose(blocks[:, :, :feat_dev], (1, 0, 2)).reshape(req_count, model_width)
    req_total = jnp.sum(blocks[:, :, feat_dev], 0)
    last_total = jnp.sum(blocks[:, :, feat_dev + 1], 0)
    req_norm = jnp.sqrt(req_total / (counts.astype(jnp.float32) * model_width) + EPS)
    last_own = (last_rows * lax.rsqrt(last_total[:, None] / model_width + EPS) * final_gain).astype(
        jnp.bfloat16
    )
    last_normed = lax.all_gather(last_own, "grp", axis=0, tiled=True)
    logits = lax.dot_general(
        last_normed, lm_head, (((1,), (1,)), ((), ())), preferred_element_type=jnp.float32
    )
    local_max = jnp.max(logits, -1)
    local_max = lax.pmax(local_max, "mdl")
    local_max = lax.pmax(local_max, "tok")
    max_logit = lax.pmax(local_max, "grp").reshape(groups_total, req_count)
    return (
        final_rows.astype(jnp.bfloat16)[None],
        appended[None],
        req_norm[None],
        max_logit,
        logits,
    )


def solution(mesh):
    return jax.shard_map(
        on_device,
        mesh=mesh,
        in_specs=(
            P("grp", "tok", "mdl"),
            P(),
            P(),
            P(),
            P(("grp", "mdl"), None, "tok", None),
            P("mdl"),
            P("mdl", "tok"),
            P("mdl", "tok"),
            P("mdl", "tok"),
            P("tok", "mdl"),
            P("mdl"),
            P("mdl", "tok"),
            P("mdl", "tok"),
            P("tok", "mdl"),
            P(),
            P(("grp", "tok", "mdl"), None),
        ),
        out_specs=(
            P("grp", "tok", "mdl"),
            P("grp", "mdl", "tok", None),
            P("grp", None),
            P(),
            P(None, ("grp", "tok", "mdl")),
        ),
        check_vma=False,
    )
```

profile of v0, /device:TPU:32, one launch (start us, length us, event | category | flops | bytes accessed | tf_op | source)
XLA Modules:
  0.0 541.8 jit_solution(11023597313740727375)
XLA Ops:
  9.2 14.9 %psum.21 = f32[128]{0:T(128)S(1)} all-reduce(f32[128]{0:T(128)S(1)} %fusion.44), channel_id=1, replica_groups=mesh['grp'=4,'tok'=8,'mdl'=8] {'mdl'}, use_global_device_ids=true, to_apply=%region_1.0 | all-reduce | flops 128 | bytes 1024 | tf_op jit(solution)/shard_map/psum | solution.py:62
  24.1 1.7 fusion.46
  25.9 38.9 %all-gather.7.cloned.1.call-done = bf16[1024,640]{1,0:T(8,128)(2,1)} async-done(((bf16[128,640]{1,0:T(8,128)(2,1)}), bf16[1024,640]{1,0:T(8,128)(2,1)}) %all-gather.7.cloned.1.call-update) | async-done | bytes 1310736 | tf_op jit(solution)/shard_map/all_gather | solution.py:68
  64.7 5.1 fusion.30
  75.3 1.6 broadcast_compare_fusion
  76.9 32.9 %reduce-scatter.5.cloned.1.call-done = f32[128,896]{0,1:T(8,128)} async-done(((f32[1024,896]{0,1:T(8,128)}), f32[128,896]{0,1:T(8,128)}) %reduce-scatter.5.cloned.1.call-update) | async-done | bytes 458768 | tf_op jit(solution)/shard_map/reduce_scatter | solution.py:72
  112.6 1.9 copy.67
  116.4 13.2 %all_gather.28 = bf16[1024,1,256]{0,2,1:T(8,128)(2,1)} all-gather(bf16[128,1,256]{0,2,1:T(8,128)(2,1)S(1)} %get-tuple-element.25), channel_id=1, replica_groups=mesh['grp'=4,'tok'=8,'mdl'=8] {'mdl'}, dimensions={0}, use_global_device_ids=true | all-gather | bytes 589824 | tf_op jit(solution)/shard_map/all_gather | solution.py:97
  129.6 1.8 subtract_convert_fusion
  131.4 13.0 %fusion = (f32[128,5]{0,1:T(8,128)S(1)}, f32[128,5,8192]{2,0,1:T(8,128)}) fusion(pred[128,8192]{1,0:T(8,128)(4,1)} %broadcast_compare_fusion, bf16[8192,1,256]{2,0,1:T(8,128)(2,1)} %bitcast.163, bf16[128,5,64]{2,0,1:T(8,128)(2,1)} %get-tuple-element.19, bf16[128,5,64]{2,0,1:T(8,128)(2,1)} %get-tuple-element.18), kind=kOutput, calls=%fused_computation.2 | convolution fusion | flops 1358232960 | bytes 24447488 | tf_op jit(solution)/shard_map/rcgd,kcd->rcgk/dot_general | solution.py:129
  144.4 2.2 fusion.10
  146.6 14.2 %fusion.21 = f32[1,128,128,5]{2,1,3,0:T(8,128)} fusion(bf16[8192,1,256]{2,0,1:T(8,128)(2,1)} %bitcast.164, f32[128,5,8192]{2,0,1:T(8,128)} %get-tuple-element.35, f32[128,5]{0,1:T(8,128)S(1)} %max.23, pred[128,8192]{1,0:T(8,128)(4,1)} %broadcast_compare_fusion), kind=kOutput, calls=%fused_computation.28 | convolution fusion | flops 1368391680 | bytes 24447488 | tf_op jit(solution)/shard_map/rcgk,kcd->rcgd/dot_general | solution.py:139
  160.8 10.7 %fusion.1 = f32[128,5]{0,1:T(8,128)S(1)} fusion(f32[128,5,8192]{2,0,1:T(8,128)} %get-tuple-element.35, f32[128,5]{0,1:T(8,128)S(1)} %max.23, pred[128,8192]{1,0:T(8,128)(4,1)} %broadcast_compare_fusion), kind=kLoop, calls=%fused_computation.3 | loop fusion | flops 26213760 | bytes 22025216 | tf_op jit(solution)/shard_map/reduce_sum | solution.py:138
  172.6 1.5 fusion.39
  174.2 27.1 %all-gather.11.cloned.1.call-done = bf16[1024,640]{0,1:T(8,128)(2,1)} async-done(((bf16[128,640]{0,1:T(8,128)(2,1)}), bf16[1024,640]{0,1:T(8,128)(2,1)}) %all-gather.11.cloned.1.call-update) | async-done | bytes 1310736 | tf_op jit(solution)/shard_map/all_gather | solution.py:151
  201.3 4.0 convolution_convert_fusion.2
  205.4 40.1 %reduce-scatter.7.cloned.1.call-done = bf16[128,640]{1,0:T(8,128)(2,1)} async-done(((bf16[1024,640]{1,0:T(8,128)(2,1)}), bf16[128,640]{1,0:T(8,128)(2,1)}) %reduce-scatter.7.cloned.1.call-update) | async-done | bytes 163856 | tf_op jit(solution)/shard_map/reduce_scatter | solution.py:155
  246.5 12.4 %psum.22 = f32[128]{0:T(128)S(1)} all-reduce(f32[128]{0:T(128)S(1)} %multiply_reduce_fusion.1), channel_id=1, replica_groups=mesh['grp'=4,'tok'=8,'mdl'=8] {'mdl'}, use_global_device_ids=true, to_apply=%region_14.15 | all-reduce | flops 128 | bytes 1024 | tf_op jit(solution)/shard_map/psum | solution.py:158
  259.0 1.7 multiply_convert_fusion
  260.7 36.0 %all-gather.13.cloned.1.call-done = bf16[1024,640]{1,0:T(8,128)(2,1)} async-done(((bf16[128,640]{1,0:T(8,128)(2,1)}), bf16[1024,640]{1,0:T(8,128)(2,1)}) %all-gather.13.cloned.1.call-update) | async-done | bytes 1310736 | tf_op jit(solution)/shard_map/all_gather | solution.py:165
  296.7 10.5 %convolution_convert_fusion = bf16[1024,3584]{1,0:T(8,128)(2,1)} fusion(bf16[1024,640]{1,0:T(8,128)(2,1)} %all-gather.13.cloned.1.call-done, bf16[640,1792]{1,0:T(8,128)(2,1)} %param.28, bf16[640,1792]{1,0:T(8,128)(2,1)} %param.27), kind=kOutput, calls=%fused_computation.8 | convolution fusion | flops 4710465536 | bytes 13238272 | tf_op jit(solution)/shard_map/dot_general | solution.py:164
  307.3 49.0 %reduce-scatter.9.cloned.1.call-done = bf16[128,3584]{1,0:T(8,128)(2,1)} async-done(((bf16[1024,3584]{1,0:T(8,128)(2,1)}), bf16[128,3584]{1,0:T(8,128)(2,1)}) %reduce-scatter.9.cloned.1.call-update) | async-done | bytes 917520 | tf_op jit(solution)/shard_map/reduce_scatter | solution.py:169
  358.8 32.2 %all-gather.15.cloned.1.call-done = bf16[1024,1792]{1,0:T(8,128)(2,1)} async-done(((bf16[128,1792]{1,0:T(8,128)(2,1)}), bf16[1024,1792]{1,0:T(8,128)(2,1)}) %all-gather.15.cloned.1.call-update) | async-done | bytes 3670032 | tf_op jit(solution)/shard_map/all_gather | solution.py:174
  390.9 6.8 %convolution_convert_fusion.1 = bf16[1024,640]{1,0:T(8,128)(2,1)} fusion(bf16[1024,1792]{1,0:T(8,128)(2,1)} %all-gather.15.cloned.1.call-done, bf16[1792,640]{1,0:T(8,128)(2,1)} %param.29), kind=kOutput, calls=%fused_computation.21 | convolution fusion | flops 2349465600 | bytes 7274496 | tf_op jit(solution)/shard_map/dot_general | solution.py:173
  398.6 38.3 %reduce-scatter.11.cloned.1.call-done = bf16[128,640]{1,0:T(8,128)(2,1)} async-done(((bf16[1024,640]{1,0:T(8,128)(2,1)}), bf16[128,640]{1,0:T(8,128)(2,1)}) %reduce-scatter.11.cloned.1.call-update) | async-done | bytes 163856 | tf_op jit(solution)/shard_map/reduce_scatter | solution.py:178
  439.4 27.0 %psum.23 = f32[1,4,642]{2,1,0:T(4,128)S(1)} all-reduce(f32[1,4,642]{2,1,0:T(4,128)S(1)} %maximum_bitcast_fusion), channel_id=1, replica_groups=mesh['grp'=4,'tok'=8,'mdl'=8] {'tok'}, use_global_device_ids=true, to_apply=%region_21.22 | all-reduce | flops 2568 | bytes 20544 | tf_op jit(solution)/shard_map/psum | solution.py:193
  466.4 13.0 %all_gather.34 = f32[8,4,642]{2,1,0:T(4,128)S(1)} all-gather(f32[1,4,642]{2,1,0:T(4,128)S(1)} %psum.23), channel_id=1, replica_groups=mesh['grp'=4,'tok'=8,'mdl'=8] {'mdl'}, dimensions={0}, use_global_device_ids=true | all-gather | bytes 92448 | tf_op jit(solution)/shard_map/all_gather | solution.py:194
  480.2 12.3 %all-gather = bf16[4,4,5120]{2,1,0:T(4,128)(2,1)S(1)} all-gather(bf16[1,4,5120]{2,1,0:T(4,128)(2,1)S(1)} %fusion.52), channel_id=1, replica_groups=mesh['grp'=4,'tok'=8,'mdl'=8] {'grp'}, dimensions={0}, use_global_device_ids=true | all-gather | bytes 204800 | tf_op jit(solution)/shard_map/all_gather | solution.py:203
  492.6 1.6 fusion.70
  494.2 12.4 %pmax.21 = f32[16]{0:T(128)S(1)} all-reduce(f32[16]{0:T(128)S(1)} %get-tuple-element.36), channel_id=1, replica_groups=mesh['grp'=4,'tok'=8,'mdl'=8] {'mdl'}, use_global_device_ids=true, to_apply=%region_25.26 | all-reduce | flops 16 | bytes 128 | tf_op jit(solution)/shard_map/pmax | solution.py:208
  506.7 16.7 %pmax.22 = f32[16]{0:T(128)S(1)} all-reduce(f32[16]{0:T(128)S(1)} %pmax.21), channel_id=1, replica_groups=mesh['grp'=4,'tok'=8,'mdl'=8] {'tok'}, use_global_device_ids=true, to_apply=%region_26.27 | all-reduce | flops 16 | bytes 128 | tf_op jit(solution)/shard_map/pmax | solution.py:209
  523.5 10.8 %pmax.23 = f32[4,4]{1,0:T(4,128)} all-reduce(f32[4,4]{1,0:T(4,128)S(1)} %reshape.478), channel_id=1, replica_groups=mesh['grp'=4,'tok'=8,'mdl'=8] {'grp'}, use_global_device_ids=true, to_apply=%region_27.28 | all-reduce | flops 16 | bytes 128 | tf_op jit(solution)/shard_map/pmax | solution.py:210
  (95 shorter events, 20.4 us)
Async XLA Ops:
  8.0 484.6 %copy-start = (bf16[300,5120]{1,0:T(8,128)(2,1)S(1)}, bf16[300,5120]{1,0:T(8,128)(2,1)}, u32[]{:S(2)}) copy-start(bf16[300,5120]{1,0:T(8,128)(2,1)} %param.31) | copy-start | bytes 9216004
  8.0 56.7 %all-gather.7.cloned.1.call-start = ((), (), s32[]{:S(2)}) async-start(), calls=%async_computation.4 | async-start | bytes 1474560 | tf_op jit(solution)/shard_map/all_gather | solution.py:68
  25.8 84.0 %reduce-scatter.5.cloned.1.call-start = ((), (), s32[]{:S(2)}) async-start(), calls=%async_computation.5 | async-start | bytes 4128768 | tf_op jit(solution)/shard_map/reduce_scatter | solution.py:72
  69.9 0.7 copy-start.11
  69.9 61.5 %all-gather.9.cloned.1.call-start = ((), (), s32[]{:S(2)}) async-start(), calls=%async_computation.6 | async-start | bytes 4325376 | tf_op jit(solution)/shard_map/all_gather | solution.py:123
  70.5 130.9 %all-gather.11.cloned.1.call-start = ((), (), s32[]{:S(2)}) async-start(), calls=%async_computation.7 | async-start | bytes 1474560 | tf_op jit(solution)/shard_map/all_gather | solution.py:151
  131.4 13.0 %copy-start.4 = (bf16[1024,1,256]{0,2,1:T(8,128)(2,1)S(1)}, bf16[1024,1,256]{0,2,1:T(8,128)(2,1)}, u32[]{:S(2)}) copy-start(bf16[1024,1,256]{0,2,1:T(8,128)(2,1)} %all_gather.28) | copy-start | bytes 1572868
  131.4 13.0 %copy-start.6 = (pred[128,1024]{0,1:T(8,128)(4,1)S(1)}, pred[128,1024]{0,1:T(8,128)(4,1)}, u32[]{:S(2)}) copy-start(pred[128,1024]{0,1:T(8,128)(4,1)} %fusion.43) | copy-start | bytes 393220
  131.4 13.0 %copy-start.7 = (bf16[128,5,64]{2,0,1:T(8,128)(2,1)S(1)}, bf16[128,5,64]{2,0,1:T(8,128)(2,1)}, u32[]{:S(2)}) copy-start(bf16[128,5,64]{2,0,1:T(8,128)(2,1)} %get-tuple-element.18) | copy-start | bytes 245764
  131.4 13.0 %copy-start.8 = (bf16[128,5,64]{2,0,1:T(8,128)(2,1)S(1)}, bf16[128,5,64]{2,0,1:T(8,128)(2,1)}, u32[]{:S(2)}) copy-start(bf16[128,5,64]{2,0,1:T(8,128)(2,1)} %get-tuple-element.19) | copy-start | bytes 245764
  160.8 10.7 %copy-start.1 = (f32[1024,128,5]{1,0,2:T(8,128)S(1)}, f32[1024,128,5]{1,0,2:T(8,128)}, u32[]{:S(2)}) copy-start(f32[1024,128,5]{1,0,2:T(8,128)} %get-tuple-element.33) | copy-start | bytes 7864324
  171.5 1.0 copy-start.5
  171.5 1.1 copy-start.12
  174.1 71.4 %copy-start.2 = (bf16[1,128,640]{2,1,0:T(8,128)(2,1)S(1)}, bf16[1,128,640]{2,1,0:T(8,128)(2,1)}, u32[]{:S(2)}) copy-start(bf16[1,128,640]{2,1,0:T(8,128)(2,1)} %param.16) | copy-start | bytes 491524
  174.1 84.8 %copy-start.10 = (f32[640]{0:T(1024)S(1)}, f32[640]{0:T(1024)}, u32[]{:S(2)}) copy-start(f32[640]{0:T(1024)} %param.26) | copy-start | bytes 7684
  174.1 71.3 %reduce-scatter.7.cloned.1.call-start = ((), (), s32[]{:S(2)}) async-start(), calls=%async_computation.8 | async-start | bytes 1474560 | tf_op jit(solution)/shard_map/reduce_scatter | solution.py:155
  205.3 91.4 %all-gather.13.cloned.1.call-start = ((), (), s32[]{:S(2)}) async-start(), calls=%async_computation.9 | async-start | bytes 1474560 | tf_op jit(solution)/shard_map/all_gather | solution.py:165
  260.7 95.6 %reduce-scatter.9.cloned.1.call-start = ((), (), s32[]{:S(2)}) async-start(), calls=%async_computation.10 | async-start | bytes 8257536 | tf_op jit(solution)/shard_map/reduce_scatter | solution.py:169
  307.2 83.7 %all-gather.15.cloned.1.call-start = ((), (), s32[]{:S(2)}) async-start(), calls=%async_computation.11 | async-start | bytes 4128768 | tf_op jit(solution)/shard_map/all_gather | solution.py:174
  358.7 78.2 %copy-start.3 = (bf16[128,640]{1,0:T(8,128)(2,1)S(1)}, bf16[128,640]{1,0:T(8,128)(2,1)}, u32[]{:S(2)}) copy-start(bf16[128,640]{1,0:T(8,128)(2,1)} %reduce-scatter.7.cloned.1.call-done) | copy-start | bytes 491524
  358.7 78.2 %reduce-scatter.11.cloned.1.call-start = ((), (), s32[]{:S(2)}) async-start(), calls=%async_computation.12 | async-start | bytes 1474560 | tf_op jit(solution)/shard_map/reduce_scatter | solution.py:178
  397.8 82.3 %copy-start.9 = (f32[5120]{0:T(1024)S(1)}, f32[5120]{0:T(1024)}, u32[]{:S(2)}) copy-start(f32[5120]{0:T(1024)} %param.30) | copy-start | bytes 61444
Sparse Core Ops, SparseCore 0:
  26.0 38.7 all-gather.6
  70.0 39.7 reduce-scatter.4
  174.2 27.0 all-gather.10
  205.4 39.9 reduce-scatter.6
  260.8 35.8 all-gather.12
  307.3 48.8 reduce-scatter.8
  358.8 32.0 all-gather.14
  397.9 38.9 reduce-scatter.10
Sparse Core Ops, SparseCore 1:
  72.9 51.0 all-gather.8
where the time goes:
time: 543 us; the launch traced here: 542 us
  waiting for transfers between devices  295 us (54%)
  blocking collectives  133 us (24%)
  matrix products  58.8 us (11%)
  other arithmetic  28.5 us (5%)
  between operations  15.8 us (3%)
  local copies, waits for them, and re-layouts  10.3 us (2%)
    reduce_scatter x1, waiting for transfers between devices, on_device(): lax.psum_scatter(partial_ffn.astype(jnp.bfloat16), 'mdl', scatter_dimensi...  49 us
    reduce_scatter x1, waiting for transfers between devices, on_device(): lax.psum_scatter(partial_out.astype(jnp.bfloat16), 'tok', scatter_dimensi...  40.1 us
    all_gather x1, waiting for transfers between devices, on_device(): lax.all_gather(normed, 'tok', axis=0, tiled=True)  38.9 us
    reduce_scatter x1, waiting for transfers between devices, on_device(): lax.psum_scatter(partial_down.astype(jnp.bfloat16), 'tok', scatter_dimens...  38.3 us
    all_gather x1, waiting for transfers between devices, on_device(): lax.all_gather(ffn_input, 'tok', axis=0, tiled=True)  36 us
    reduce_scatter x1, waiting for transfers between devices, on_device(): lax.psum_scatter(partial_qkv, 'mdl', scatter_dimension=0, tiled=True)  32.9 us
    all_gather x1, waiting for transfers between devices, on_device(): lax.all_gather(activated, 'mdl', axis=0, tiled=True)  32.2 us
    all_gather x1, waiting for transfers between devices, on_device(): lax.all_gather(attended, 'mdl', axis=0, tiled=True)  27.1 us
  transfers between devices with their start and end apart: 9, of which 8 were waited for; matrix products, arithmetic and copies ran while one was open for 3% of the time, Pallas kernels for 0%

commit v1 on v0

--- a/solution.py
+++ b/solution.py
@@ -8,6 +8,11 @@
 EPS = 1e-06
 THETA = 1000000.0
 NEG = -1e30
+
+
+def tiled_gather(x, axis, dim):
+    copies = jnp.concatenate([x] * lax.axis_size(axis), axis=dim)
+    return lax.all_to_all(copies, axis, dim, dim, tiled=True)
 
 
 def rotate(tensor, positions):
@@ -162,9 +167,7 @@
     w_pair = jnp.concatenate([w_gate, w_up], 1)
     ff_dev = w_gate.shape[1]
     partial_ffn = jnp.dot(
-        lax.all_gather(ffn_input, "tok", axis=0, tiled=True),
-        w_pair,
-        preferred_element_type=jnp.float32,
+        tiled_gather(ffn_input, "tok", 0), w_pair, preferred_element_type=jnp.float32
     )
     summed = lax.psum_scatter(
         partial_ffn.astype(jnp.bfloat16), "mdl", scatter_dimension=0, tiled=True

time: 543 us -> 538 us (level)
  waiting for transfers between devices: 295 us -> 255 us
  blocking collectives: 133 us -> 171 us
    all_to_all x0 -> x1, blocking collectives: none -> 38.5 us  [tiled_gather(): return lax.all_to_all(copies, axis, dim, dim, tiled=True)]
    all_gather x1 -> x0, waiting for transfers between devices: 36 us -> none  [on_device(): lax.all_gather(ffn_input, 'tok', axis=0, tiled=True)]
  transfers between devices with their start and end apart: 9 -> 8, of which waited for: 8 -> 7; matrix products, arithmetic and copies ran while one was open for 3% -> 3% of each run, Pallas kernels for 0% -> 0%
where the time goes in v1:
time: 538 us; the launch traced here: 537 us
  waiting for transfers between devices  255 us (47%)
  blocking collectives  171 us (32%)
  matrix products  56.5 us (11%)
  other arithmetic  27.9 us (5%)
  between operations  15.9 us (3%)
  local copies, waits for them, and re-layouts  10.5 us (2%)
    reduce_scatter x1, waiting for transfers between devices, on_device(): lax.psum_scatter(partial_ffn.astype(jnp.bfloat16), 'mdl', scatter_dimensi...  44.9 us
    reduce_scatter x1, waiting for transfers between devices, on_device(): lax.psum_scatter(partial_out.astype(jnp.bfloat16), 'tok', scatter_dimensi...  40.1 us
    all_gather x1, waiting for transfers between devices, on_device(): lax.all_gather(normed, 'tok', axis=0, tiled=True)  38.9 us
    all_to_all x1, blocking collectives, tiled_gather(): return lax.all_to_all(copies, axis, dim, dim, tiled=True)  38.5 us
    reduce_scatter x1, waiting for transfers between devices, on_device(): lax.psum_scatter(partial_down.astype(jnp.bfloat16), 'tok', scatter_dimens...  38.3 us
    reduce_scatter x1, waiting for transfers between devices, on_device(): lax.psum_scatter(partial_qkv, 'mdl', scatter_dimension=0, tiled=True)  32.9 us
    all_gather x1, waiting for transfers between devices, on_device(): lax.all_gather(activated, 'mdl', axis=0, tiled=True)  32.2 us
    all_gather x1, waiting for transfers between devices, on_device(): lax.all_gather(attended, 'mdl', axis=0, tiled=True)  27.1 us
  transfers between devices with their start and end apart: 8, of which 7 were waited for; matrix products, arithmetic and copies ran while one was open for 3% of the time, Pallas kernels for 0%

profile of v1, /device:TPU:32, one launch (start us, length us, event | category | flops | bytes accessed | tf_op | source)
XLA Modules:
  0.0 537.2 jit_solution(7645066216428883610)
XLA Ops:
  9.2 14.9 %psum.21 = f32[128]{0:T(128)S(1)} all-reduce(f32[128]{0:T(128)S(1)} %fusion.44), channel_id=1, replica_groups=mesh['grp'=4,'tok'=8,'mdl'=8] {'mdl'}, use_global_device_ids=true, to_apply=%region_1.0 | all-reduce | flops 128 | bytes 1024 | tf_op jit(solution)/shard_map/psum | solution.py:67
  24.1 1.7 fusion.46
  25.9 38.9 %all-gather.6.cloned.1.call-done = bf16[1024,640]{1,0:T(8,128)(2,1)} async-done(((bf16[128,640]{1,0:T(8,128)(2,1)}), bf16[1024,640]{1,0:T(8,128)(2,1)}) %all-gather.6.cloned.1.call-update) | async-done | bytes 1310736 | tf_op jit(solution)/shard_map/all_gather | solution.py:73
  64.7 5.1 fusion.30
  75.3 1.6 broadcast_compare_fusion
  76.9 32.9 %reduce-scatter.5.cloned.1.call-done = f32[128,896]{0,1:T(8,128)} async-done(((f32[1024,896]{0,1:T(8,128)}), f32[128,896]{0,1:T(8,128)}) %reduce-scatter.5.cloned.1.call-update) | async-done | bytes 458768 | tf_op jit(solution)/shard_map/reduce_scatter | solution.py:77
  112.6 1.9 copy.67
  116.4 13.2 %all_gather.25 = bf16[1024,1,256]{0,2,1:T(8,128)(2,1)} all-gather(bf16[128,1,256]{0,2,1:T(8,128)(2,1)S(1)} %get-tuple-element.27), channel_id=1, replica_groups=mesh['grp'=4,'tok'=8,'mdl'=8] {'mdl'}, dimensions={0}, use_global_device_ids=true | all-gather | bytes 589824 | tf_op jit(solution)/shard_map/all_gather | solution.py:102
  129.6 1.8 subtract_convert_fusion
  131.4 13.0 %fusion = (f32[128,5]{0,1:T(8,128)S(1)}, f32[128,5,8192]{2,0,1:T(8,128)}) fusion(pred[128,8192]{1,0:T(8,128)(4,1)} %broadcast_compare_fusion, bf16[8192,1,256]{2,0,1:T(8,128)(2,1)} %bitcast.168, bf16[128,5,64]{2,0,1:T(8,128)(2,1)} %get-tuple-element.21, bf16[128,5,64]{2,0,1:T(8,128)(2,1)} %get-tuple-element.20), kind=kOutput, calls=%fused_computation.2 | convolution fusion | flops 1358232960 | bytes 24447488 | tf_op jit(solution)/shard_map/rcgd,kcd->rcgk/dot_general | solution.py:134
  144.4 2.2 fusion.10
  146.6 14.2 %fusion.21 = f32[1,128,128,5]{2,1,3,0:T(8,128)} fusion(bf16[8192,1,256]{2,0,1:T(8,128)(2,1)} %bitcast.169, f32[128,5,8192]{2,0,1:T(8,128)} %get-tuple-element.37, f32[128,5]{0,1:T(8,128)S(1)} %max.23, pred[128,8192]{1,0:T(8,128)(4,1)} %broadcast_compare_fusion), kind=kOutput, calls=%fused_computation.28 | convolution fusion | flops 1368391680 | bytes 24447488 | tf_op jit(solution)/shard_map/rcgk,kcd->rcgd/dot_general | solution.py:144
  160.8 10.7 %fusion.1 = f32[128,5]{0,1:T(8,128)S(1)} fusion(f32[128,5,8192]{2,0,1:T(8,128)} %get-tuple-element.37, f32[128,5]{0,1:T(8,128)S(1)} %max.23, pred[128,8192]{1,0:T(8,128)(4,1)} %broadcast_compare_fusion), kind=kLoop, calls=%fused_computation.3 | loop fusion | flops 26213760 | bytes 22025216 | tf_op jit(solution)/shard_map/reduce_sum | solution.py:143
  172.6 1.5 fusion.39
  174.2 27.1 %all-gather.10.cloned.1.call-done = bf16[1024,640]{0,1:T(8,128)(2,1)} async-done(((bf16[128,640]{0,1:T(8,128)(2,1)}), bf16[1024,640]{0,1:T(8,128)(2,1)}) %all-gather.10.cloned.1.call-update) | async-done | bytes 1310736 | tf_op jit(solution)/shard_map/all_gather | solution.py:156
  201.3 4.0 convolution_convert_fusion.2
  205.4 40.1 %reduce-scatter.7.cloned.1.call-done = bf16[128,640]{1,0:T(8,128)(2,1)} async-done(((bf16[1024,640]{1,0:T(8,128)(2,1)}), bf16[128,640]{1,0:T(8,128)(2,1)}) %reduce-scatter.7.cloned.1.call-update) | async-done | bytes 163856 | tf_op jit(solution)/shard_map/reduce_scatter | solution.py:160
  246.5 12.4 %psum.22 = f32[128]{0:T(128)S(1)} all-reduce(f32[128]{0:T(128)S(1)} %multiply_reduce_fusion.1), channel_id=1, replica_groups=mesh['grp'=4,'tok'=8,'mdl'=8] {'mdl'}, use_global_device_ids=true, to_apply=%region_14.15 | all-reduce | flops 128 | bytes 1024 | tf_op jit(solution)/shard_map/psum | solution.py:163
  260.2 38.5 %all_to_all.12 = bf16[8,128,640]{2,1,0:T(8,128)(2,1)S(1)} all-to-all(bf16[8,128,640]{2,1,0:T(8,128)(2,1)S(1)} %bitcast.157), channel_id=1, replica_groups=mesh['grp'=4,'tok'=8,'mdl'=8] {'tok'}, dimensions={0} | all-to-all | bytes 2621440 | tf_op jit(solution)/shard_map/all_to_all | solution.py:15
  298.7 8.1 %convolution_convert_fusion = bf16[1024,3584]{1,0:T(8,128)(2,1)} fusion(bf16[1024,640]{1,0:T(8,128)(2,1)S(1)} %bitcast.158, bf16[640,1792]{1,0:T(8,128)(2,1)S(1)} %copy-done.11, bf16[640,1792]{1,0:T(8,128)(2,1)S(1)} %copy-done.12), kind=kOutput, calls=%fused_computation.8 | convolution fusion | flops 4710465536 | bytes 13238272 | tf_op jit(solution)/shard_map/dot_general | solution.py:169
  306.9 44.9 %reduce-scatter.9.cloned.1.call-done = bf16[128,3584]{1,0:T(8,128)(2,1)} async-done(((bf16[1024,3584]{1,0:T(8,128)(2,1)}), bf16[128,3584]{1,0:T(8,128)(2,1)}) %reduce-scatter.9.cloned.1.call-update) | async-done | bytes 917520 | tf_op jit(solution)/shard_map/reduce_scatter | solution.py:172
  351.8 1.4 convert_element_type.104
  354.3 32.2 %all-gather.12.cloned.1.call-done = bf16[1024,1792]{1,0:T(8,128)(2,1)} async-done(((bf16[128,1792]{1,0:T(8,128)(2,1)}), bf16[1024,1792]{1,0:T(8,128)(2,1)}) %all-gather.12.cloned.1.call-update) | async-done | bytes 3670032 | tf_op jit(solution)/shard_map/all_gather | solution.py:177
  386.4 6.8 %convolution_convert_fusion.1 = bf16[1024,640]{1,0:T(8,128)(2,1)} fusion(bf16[1024,1792]{1,0:T(8,128)(2,1)} %all-gather.12.cloned.1.call-done, bf16[1792,640]{1,0:T(8,128)(2,1)} %param.29), kind=kOutput, calls=%fused_computation.21 | convolution fusion | flops 2349465600 | bytes 7274496 | tf_op jit(solution)/shard_map/dot_general | solution.py:176
  394.1 38.3 %reduce-scatter.11.cloned.1.call-done = bf16[128,640]{1,0:T(8,128)(2,1)} async-done(((bf16[1024,640]{1,0:T(8,128)(2,1)}), bf16[128,640]{1,0:T(8,128)(2,1)}) %reduce-scatter.11.cloned.1.call-update) | async-done | bytes 163856 | tf_op jit(solution)/shard_map/reduce_scatter | solution.py:181
  434.8 27.0 %psum.23 = f32[1,4,642]{2,1,0:T(4,128)S(1)} all-reduce(f32[1,4,642]{2,1,0:T(4,128)S(1)} %maximum_bitcast_fusion), channel_id=1, replica_groups=mesh['grp'=4,'tok'=8,'mdl'=8] {'tok'}, use_global_device_ids=true, to_apply=%region_21.22 | all-reduce | flops 2568 | bytes 20544 | tf_op jit(solution)/shard_map/psum | solution.py:196
  461.8 13.0 %all_gather.30 = f32[8,4,642]{2,1,0:T(4,128)S(1)} all-gather(f32[1,4,642]{2,1,0:T(4,128)S(1)} %psum.23), channel_id=1, replica_groups=mesh['grp'=4,'tok'=8,'mdl'=8] {'mdl'}, dimensions={0}, use_global_device_ids=true | all-gather | bytes 92448 | tf_op jit(solution)/shard_map/all_gather | solution.py:197
  475.7 12.3 %all-gather = bf16[4,4,5120]{2,1,0:T(4,128)(2,1)S(1)} all-gather(bf16[1,4,5120]{2,1,0:T(4,128)(2,1)S(1)} %fusion.52), channel_id=1, replica_groups=mesh['grp'=4,'tok'=8,'mdl'=8] {'grp'}, dimensions={0}, use_global_device_ids=true | all-gather | bytes 204800 | tf_op jit(solution)/shard_map/all_gather | solution.py:206
  488.1 1.6 fusion.70
  489.8 12.4 %pmax.21 = f32[16]{0:T(128)S(1)} all-reduce(f32[16]{0:T(128)S(1)} %get-tuple-element.38), channel_id=1, replica_groups=mesh['grp'=4,'tok'=8,'mdl'=8] {'mdl'}, use_global_device_ids=true, to_apply=%region_25.26 | all-reduce | flops 16 | bytes 128 | tf_op jit(solution)/shard_map/pmax | solution.py:211
  502.2 16.7 %pmax.22 = f32[16]{0:T(128)S(1)} all-reduce(f32[16]{0:T(128)S(1)} %pmax.21), channel_id=1, replica_groups=mesh['grp'=4,'tok'=8,'mdl'=8] {'tok'}, use_global_device_ids=true, to_apply=%region_26.27 | all-reduce | flops 16 | bytes 128 | tf_op jit(solution)/shard_map/pmax | solution.py:212
  519.0 10.8 %pmax.23 = f32[4,4]{1,0:T(4,128)} all-reduce(f32[4,4]{1,0:T(4,128)S(1)} %reshape.480), channel_id=1, replica_groups=mesh['grp'=4,'tok'=8,'mdl'=8] {'grp'}, use_global_device_ids=true, to_apply=%region_27.28 | all-reduce | flops 16 | bytes 128 | tf_op jit(solution)/shard_map/pmax | solution.py:213
  (104 shorter events, 20.2 us)
Async XLA Ops:
  8.0 480.1 %copy-start = (bf16[300,5120]{1,0:T(8,128)(2,1)S(1)}, bf16[300,5120]{1,0:T(8,128)(2,1)}, u32[]{:S(2)}) copy-start(bf16[300,5120]{1,0:T(8,128)(2,1)} %param.31) | copy-start | bytes 9216004
  8.0 56.7 %all-gather.6.cloned.1.call-start = ((), (), s32[]{:S(2)}) async-start(), calls=%async_computation.5 | async-start | bytes 1474560 | tf_op jit(solution)/shard_map/all_gather | solution.py:73
  25.8 84.0 %reduce-scatter.5.cloned.1.call-start = ((), (), s32[]{:S(2)}) async-start(), calls=%async_computation.6 | async-start | bytes 4128768 | tf_op jit(solution)/shard_map/reduce_scatter | solution.py:77
  69.9 0.7 copy-start.13
  69.9 61.5 %all-gather.8.cloned.1.call-start = ((), (), s32[]{:S(2)}) async-start(), calls=%async_computation.7 | async-start | bytes 4325376 | tf_op jit(solution)/shard_map/all_gather | solution.py:128
  70.5 130.9 %all-gather.10.cloned.1.call-start = ((), (), s32[]{:S(2)}) async-start(), calls=%async_computation.8 | async-start | bytes 1474560 | tf_op jit(solution)/shard_map/all_gather | solution.py:156
  131.4 13.0 %copy-start.4 = (bf16[1024,1,256]{0,2,1:T(8,128)(2,1)S(1)}, bf16[1024,1,256]{0,2,1:T(8,128)(2,1)}, u32[]{:S(2)}) copy-start(bf16[1024,1,256]{0,2,1:T(8,128)(2,1)} %all_gather.25) | copy-start | bytes 1572868
  131.4 13.0 %copy-start.6 = (pred[128,1024]{0,1:T(8,128)(4,1)S(1)}, pred[128,1024]{0,1:T(8,128)(4,1)}, u32[]{:S(2)}) copy-start(pred[128,1024]{0,1:T(8,128)(4,1)} %fusion.43) | copy-start | bytes 393220
  131.4 13.0 %copy-start.7 = (bf16[128,5,64]{2,0,1:T(8,128)(2,1)S(1)}, bf16[128,5,64]{2,0,1:T(8,128)(2,1)}, u32[]{:S(2)}) copy-start(bf16[128,5,64]{2,0,1:T(8,128)(2,1)} %get-tuple-element.20) | copy-start | bytes 245764
  131.4 13.0 %copy-start.8 = (bf16[128,5,64]{2,0,1:T(8,128)(2,1)S(1)}, bf16[128,5,64]{2,0,1:T(8,128)(2,1)}, u32[]{:S(2)}) copy-start(bf16[128,5,64]{2,0,1:T(8,128)(2,1)} %get-tuple-element.21) | copy-start | bytes 245764
  160.8 10.7 %copy-start.1 = (f32[1024,128,5]{1,0,2:T(8,128)S(1)}, f32[1024,128,5]{1,0,2:T(8,128)}, u32[]{:S(2)}) copy-start(f32[1024,128,5]{1,0,2:T(8,128)} %get-tuple-element.35) | copy-start | bytes 7864324
  171.5 1.0 copy-start.5
  171.5 1.1 copy-start.14
  174.1 71.4 %copy-start.2 = (bf16[1,128,640]{2,1,0:T(8,128)(2,1)S(1)}, bf16[1,128,640]{2,1,0:T(8,128)(2,1)}, u32[]{:S(2)}) copy-start(bf16[1,128,640]{2,1,0:T(8,128)(2,1)} %param.16) | copy-start | bytes 491524
  174.1 84.8 %copy-start.10 = (f32[640]{0:T(1024)S(1)}, f32[640]{0:T(1024)}, u32[]{:S(2)}) copy-start(f32[640]{0:T(1024)} %param.26) | copy-start | bytes 7684
  174.1 71.3 %reduce-scatter.7.cloned.1.call-start = ((), (), s32[]{:S(2)}) async-start(), calls=%async_computation.9 | async-start | bytes 1474560 | tf_op jit(solution)/shard_map/reduce_scatter | solution.py:160
  205.3 146.5 %reduce-scatter.9.cloned.1.call-start = ((), (), s32[]{:S(2)}) async-start(), calls=%async_computation.10 | async-start | bytes 8257536 | tf_op jit(solution)/shard_map/reduce_scatter | solution.py:172
  260.0 38.7 %copy-start.11 = (bf16[640,1792]{1,0:T(8,128)(2,1)S(1)}, bf16[640,1792]{1,0:T(8,128)(2,1)}, u32[]{:S(2)}) copy-start(bf16[640,1792]{1,0:T(8,128)(2,1)} %param.28) | copy-start | bytes 6881284
  260.0 38.7 %copy-start.12 = (bf16[640,1792]{1,0:T(8,128)(2,1)S(1)}, bf16[640,1792]{1,0:T(8,128)(2,1)}, u32[]{:S(2)}) copy-start(bf16[640,1792]{1,0:T(8,128)(2,1)} %param.27) | copy-start | bytes 6881284
  306.8 79.6 %all-gather.12.cloned.1.call-start = ((), (), s32[]{:S(2)}) async-start(), calls=%async_computation.11 | async-start | bytes 4128768 | tf_op jit(solution)/shard_map/all_gather | solution.py:177
  354.2 78.2 %copy-start.3 = (bf16[128,640]{1,0:T(8,128)(2,1)S(1)}, bf16[128,640]{1,0:T(8,128)(2,1)}, u32[]{:S(2)}) copy-start(bf16[128,640]{1,0:T(8,128)(2,1)} %reduce-scatter.7.cloned.1.call-done) | copy-start | bytes 491524
  354.2 78.2 %reduce-scatter.11.cloned.1.call-start = ((), (), s32[]{:S(2)}) async-start(), calls=%async_computation.12 | async-start | bytes 1474560 | tf_op jit(solution)/shard_map/reduce_scatter | solution.py:181
  393.3 82.4 %copy-start.9 = (f32[5120]{0:T(1024)S(1)}, f32[5120]{0:T(1024)}, u32[]{:S(2)}) copy-start(f32[5120]{0:T(1024)} %param.30) | copy-start | bytes 61444
Sparse Core Ops, SparseCore 0:
  26.0 38.7 all-gather.5
  70.0 39.7 reduce-scatter.4
  174.2 27.0 all-gather.9
  205.4 39.9 reduce-scatter.6
  307.0 44.7 reduce-scatter.8
  354.3 32.0 all-gather.11
  393.4 38.9 reduce-scatter.10
Sparse Core Ops, SparseCore 1:
  72.9 51.0 all-gather.7
